TPU v7x, 32 devices: a whole 2x2x4 slice. The times are simulated.
32 devices in a mesh: fsdp: 8 (over z, y), rows: 4 (over x, core).
Axes of the slice: x: 2, y: 2, z: 4, core: 2. Of those that a mesh axis runs over, the one named last changes fastest.
Arguments:
- frames: bfloat16 [8, 12, 16, 1536], P('fsdp', 'rows'), may hold values from -6 to 6
- kernel: float32 [7, 7, 1536], replicated, may hold values from -0.875 to 0.875
- kernel_bias: float32 [1536], replicated, may hold values from -3 to 3
- layer_norm_weight: float32 [1536], replicated, may hold values from 0.25 to 1.75
- layer_norm_bias: float32 [1536], replicated, may hold values from -3 to 3
- up_weight: bfloat16 [1536, 6144], P('fsdp', 'rows'), may hold values from -1 to 1, as said below
- up_bias: float32 [6144], P('rows'), may hold values from -3 to 3
- grn_gamma: float32 [6144], P('rows'), may hold values from 0.2 to 1
- grn_beta: float32 [6144], P('rows'), may hold values from -3 to 3
- grad_out: bfloat16 [8, 12, 16, 6144], P('fsdp', None, None, 'rows'), may hold values from -8 to 8, as said below
Outputs:
- activation: bfloat16 [8, 12, 16, 6144], P('fsdp', None, None, 'rows')
- frames_grad: bfloat16 [8, 12, 16, 1536], P('fsdp', 'rows')
- up_weight_grad: float32 [1536, 6144], P('fsdp', 'rows')
- kernel_grad: float32 [7, 7, 1536], replicated
Inputs may be any that keep to these rules, and one draw needn't show every extreme that they name: `up_weight`: entries lie within the bounds. `grad_out`: entries lie within the bounds.
All inputs are finite; a program needn't handle non-finite values.
Results may differ from a plain program's by a relative error of at most 0.014.
Values may be sent and summed in bfloat16 or wider, within the bound.
No kernel may reach another device: no remote copies, remote signals or barrier semaphores. Data moves between devices by JAX's collectives and lax.ppermute only.
A program may use at most 64 MiB of HBM per device.

v0:
```python
import jax
import jax.numpy as jnp
from jax import lax
from jax.sharding import PartitionSpec as P

FF = 6144


def extended(block, sides, width):
    for axis, dim in sides:
        count = lax.axis_size(axis)
        forward = [(i, i + 1) for i in range(count - 1)]
        backward = [(target, source) for source, target in forward]
        low = lax.ppermute(
            lax.slice_in_dim(block, block.shape[dim] - width, None, axis=dim), axis, forward
        )
        high = lax.ppermute(lax.slice_in_dim(block, 0, width, axis=dim), axis, backward)
        block = jnp.concatenate([low, block, high], axis=dim)
    return block


def conv_rows(framed, kern, kbias):
    rows = framed.shape[0] - 6
    cols = framed.shape[1]
    wide = jnp.pad(framed, ((0, 0), (3, 3), (0, 0)))
    total = jnp.zeros((rows, cols, framed.shape[2]), jnp.float32) + kbias
    for i in range(kern.shape[0]):
        for j in range(kern.shape[1]):
            total = total + wide[i : i + rows, j : j + cols].astype(jnp.float32) * kern[i, j]
    return total


def back_conv(grad_pad, kern):
    rows = grad_pad.shape[0] - 6
    cols = grad_pad.shape[1]
    wide = jnp.pad(grad_pad, ((0, 0), (3, 3), (0, 0)))
    total = jnp.zeros((rows, cols, grad_pad.shape[2]), jnp.float32)
    for i in range(kern.shape[0]):
        for j in range(kern.shape[1]):
            total = (
                total
                + wide[6 - i : 6 - i + rows, 6 - j : 6 - j + cols].astype(jnp.float32) * kern[i, j]
            )
    return total


def kern_grad(framed, grad_rows):
    rows = grad_rows.shape[0]
    cols = grad_rows.shape[1]
    wide = jnp.pad(framed, ((0, 0), (3, 3), (0, 0)))
    grad_f = grad_rows.astype(jnp.float32)
    parts = []
    for i in range(7):
        for j in range(7):
            parts.append(
                jnp.sum(wide[i : i + rows, j : j + cols].astype(jnp.float32) * grad_f, axis=(0, 1))
            )
    return jnp.stack(parts).reshape(7, 7, grad_rows.shape[2])


def apply_layer_norm(activation_rows, scale_factor, offset_bias):
    centered_input = activation_rows - jnp.mean(activation_rows, axis=-1, keepdims=True)
    inverse_deviation = lax.rsqrt(
        jnp.mean(centered_input * centered_input, axis=-1, keepdims=True) + 1e-06
    )
    standardized_input = centered_input * inverse_deviation
    return (
        (standardized_input * scale_factor + offset_bias).astype(jnp.bfloat16),
        standardized_input,
        inverse_deviation,
    )


def gelu_grad(value):
    return (
        0.5 * (1.0 + jax.scipy.special.erf(value * 0.7071067811865476))
        + value * jnp.exp(-0.5 * value * value) * 0.3989422804014327
    )


def layer_norm_backward(normed_input_gradient, scale_factor, standardized_input, inverse_deviation):
    scaled_output = normed_input_gradient * scale_factor
    return (
        inverse_deviation
        * (
            scaled_output
            - jnp.mean(scaled_output, axis=-1, keepdims=True)
            - standardized_input
            * jnp.mean(scaled_output * standardized_input, axis=-1, keepdims=True)
        )
    ).astype(jnp.bfloat16)


def body(
    frames,
    kernel,
    kernel_bias,
    layer_norm_weight,
    layer_norm_bias,
    up_weight,
    up_bias,
    grn_gamma,
    grn_beta,
    grad_out,
):
    slab = frames[0]
    chans = slab.shape[2]
    columns = lax.all_gather(up_weight, "fsdp", axis=0, tiled=True)
    padded = extended(slab, (("rows", 0),), 3)
    activation_rows = conv_rows(padded, kernel, kernel_bias)
    normed_output, standardized_input, inverse_deviation = apply_layer_norm(
        activation_rows, layer_norm_weight, layer_norm_bias
    )
    whole = lax.all_gather(normed_output, "rows", axis=0, tiled=True)
    height = whole.shape[0]
    cols = whole.shape[1]
    flat = whole.reshape(-1, chans)
    pre = jnp.dot(flat, columns, preferred_element_type=jnp.float32) + up_bias
    post = jax.nn.gelu(pre, approximate=False)
    norms = jnp.sqrt(jnp.sum(post * post, axis=0) + 1e-06)
    cot_f = grad_out[0].reshape(flat.shape[0], -1).astype(jnp.float32)
    dnorm = grn_gamma * jnp.sum(cot_f * post, axis=0)
    norm_total = lax.psum(jnp.sum(norms), "rows")
    denom = norm_total / FF + 1e-06
    ratio = norms / denom
    output = (grn_gamma * (post * ratio) + grn_beta + post).astype(jnp.bfloat16)
    cross = lax.psum(jnp.sum(dnorm * norms), "rows")
    dnorms = dnorm / denom - cross / (denom * denom) / FF
    dpost = cot_f * (1.0 + grn_gamma * ratio) + post * (dnorms / norms)
    dpre = (dpost * gelu_grad(pre)).astype(jnp.bfloat16)
    w_term = lax.dot_general(
        flat, dpre, (((0,), (0,)), ((), ())), preferred_element_type=jnp.float32
    )
    up_grad = lax.psum_scatter(
        w_term.astype(jnp.bfloat16), "fsdp", scatter_dimension=0, tiled=True
    ).astype(jnp.float32)
    dpre_rows = dpre.reshape(height, cols, -1)
    normed_input_gradient = lax.psum_scatter(
        jnp.einsum("hwf,cf->hwc", dpre_rows, columns, preferred_element_type=jnp.float32).astype(
            jnp.bfloat16
        ),
        "rows",
        scatter_dimension=0,
        tiled=True,
    ).astype(jnp.float32)
    activation_gradient = layer_norm_backward(
        normed_input_gradient, layer_norm_weight, standardized_input, inverse_deviation
    )
    grad_pad = extended(activation_gradient, (("rows", 0),), 3)
    dframe = back_conv(grad_pad, kernel).astype(jnp.bfloat16)
    kernel_local = kern_grad(padded, activation_gradient)
    kernel_total = lax.psum(kernel_local, ("fsdp", "rows"))
    activation = output.reshape(1, height, cols, -1)
    return (activation, dframe.reshape((1,) + dframe.shape), up_grad, kernel_total)


def solution(mesh):
    placed = (
        P("fsdp", "rows", None, None),
        P(),
        P(),
        P(),
        P(),
        P("fsdp", "rows"),
        P("rows"),
        P("rows"),
        P("rows"),
        P("fsdp", None, None, "rows"),
    )
    return jax.shard_map(
        body,
        mesh=mesh,
        in_specs=placed,
        out_specs=(
            P("fsdp", None, None, "rows"),
            P("fsdp", "rows", None, None),
            P("fsdp", "rows"),
            P(),
        ),
        check_vma=False,
    )
```

profile of v0, /device:TPU:1, one launch (start us, length us, event | category | flops | bytes accessed | tf_op | source)
XLA Modules:
  0.0 376.6 jit_solution(9324311914852352310)
XLA Ops:
  7.2 0.0 all-gather.2.cloned.1.call-start
  7.2 0.7 all-gather.2.cloned.1.call-update
  7.9 0.0 reduce-scatter.3.cloned.1.call-start
  8.0 2.0 collective-permute-start.1
  9.9 4.5 %collective-permute-start = (bf16[3,16,1536]{2,1,0:T(8,128)(2,1)}, bf16[3,16,1536]{2,1,0:T(8,128)(2,1)S(1)}, u32[]{:S(2)}, u32[]{:S(2)}) collective-permute-start(bf16[3,16,1536]{2,1,0:T(8,128)(2,1)} %bitcast.25), channel_id=1, source_target_pairs={{0,1},{1,2},{2,3},{4,5},{5,6},{6,7},{8,9},{9,10},{10,11},{12,13},{... | collective-permute-start | bytes 442376 | tf_op jit(solution)/shard_map/ppermute | solution.py:14
  14.4 2.0 slice_reduce_fusion.48
  16.4 1.3 slice_reduce_fusion.46
  17.7 0.0 copy-start.4
  17.7 1.8 slice_reduce_fusion.47
  19.7 0.2 select_maximum_fusion.2
  20.0 0.0 copy-start.3
  20.0 0.0 copy-start.50
  20.0 3.4 fusion.158
  23.6 0.0 copy-start.1
  23.6 0.0 copy-start.53
  23.6 0.2 multiply_reduce_fusion.2
  23.8 0.4 copy-done.46
  24.2 0.6 copy-done.48
  24.8 0.1 add_convert_fusion.1
  24.9 6.9 %all_gather.6 = bf16[12,16,1536]{2,1,0:T(8,128)(2,1)S(1)} all-gather(bf16[3,16,1536]{2,1,0:T(8,128)(2,1)S(1)} %add_convert_fusion.1), channel_id=1, replica_groups=mesh['fsdp'=8,'rows'=4] {'rows'}, dimensions={0}, use_global_device_ids=true | all-gather | bytes 737280 | tf_op jit(solution)/shard_map/all_gather | solution.py:114
  31.8 59.4 %all-gather.2.cloned.1.call-done = bf16[1536,1536]{1,0:T(8,128)(2,1)} async-done(((bf16[192,1536]{1,0:T(8,128)(2,1)}), bf16[1536,1536]{1,0:T(8,128)(2,1)}) %all-gather.2.cloned.1.call-update) | async-done | bytes 4718608 | tf_op jit(solution)/shard_map/all_gather | solution.py:108
  91.2 7.3 %fusion.9 = (f32[1536]{0:T(1024)S(1)}, f32[1536]{0:T(1024)S(1)}, f32[192,1536]{1,0:T(8,128)}, f32[192,1536]{1,0:T(8,128)}) fusion(bf16[1,12,16,1536]{3,2,1,0:T(8,128)(2,1)S(1)} %copy-done.1, f32[1536]{0:T(1024)S(1)} %copy-done.53, bf16[192,1536]{1,0:T(8,128)(2,1)S(1)} %bitcast.21, bf16[1536,1536]{1,0:T(8,128)(2,1)} %all-gather.2.cloned.1.call-done), kind=kOutput, calls=%fused_computation.65 | convolution fusion | flops 926610432 | bytes 8275968 | tf_op jit(solution)/shard_map/dot_general | solution.py:118
  98.6 0.7 multiply_reduce_fusion.3
  99.2 7.3 %all-reduce.2 = (f32[]{:T(128)}, f32[]{:T(128)}) all-reduce(f32[]{:T(128)} %get-tuple-element.115, f32[]{:T(128)} %get-tuple-element.114), channel_id=1, replica_groups=mesh['fsdp'=8,'rows'=4] {'rows'}, use_global_device_ids=true, to_apply=%region_4.5 | all-reduce | flops 2 | bytes 16 | tf_op jit(solution)/shard_map/psum | solution.py:123
  107.9 3.2 fusion.8
  111.1 4.8 %fusion.2 = bf16[12,16,1536]{2,1,0:T(8,128)(2,1)} fusion(bf16[12,16,1536]{2,1,0:T(8,128)(2,1)S(1)} %bitcast.23, bf16[1536,1536]{1,0:T(8,128)(2,1)} %all-gather.2.cloned.1.call-done), kind=kOutput, calls=%fused_computation.54 | convolution fusion | flops 906264576 | bytes 5898240 | tf_op jit(solution)/shard_map/hwf,cf->hwc/dot_general | solution.py:139
  116.0 0.0 reduce-scatter.3.cloned.1.call-update
  116.0 0.0 reduce-scatter.5.cloned.1.call-start
  116.0 3.6 convolution_convert_fusion
  119.6 0.0 reduce-scatter.5.cloned.1.call-update
  119.6 0.0 all-reduce.5.cloned.1.call-start
  119.7 16.9 %reduce-scatter.3.cloned.1.call-done = bf16[3,16,1536]{2,1,0:T(8,128)(2,1)} async-done(((bf16[12,16,1536]{2,1,0:T(8,128)(2,1)}), bf16[3,16,1536]{2,1,0:T(8,128)(2,1)}) %reduce-scatter.3.cloned.1.call-update) | async-done | bytes 147472 | tf_op jit(solution)/shard_map/reduce_scatter | solution.py:138
  136.6 1.1 fusion.147
  137.7 1.9 fusion.145
  139.6 2.8 collective-permute-start.3
  142.3 3.0 collective-permute-start.2
  145.3 0.8 fusion.146
  146.1 0.6 fusion.136
  147.4 0.5 stack.199
  147.9 0.0 copy-start.5
  148.1 0.8 reshape.62
  148.9 0.0 all-reduce.5.cloned.1.call-update
  148.9 0.2 select_maximum_fusion
  149.3 2.8 fusion.153
  152.1 83.8 %reduce-scatter.5.cloned.1.call-done = bf16[192,1536]{1,0:T(8,128)(2,1)} async-done(((bf16[1536,1536]{1,0:T(8,128)(2,1)}), bf16[192,1536]{1,0:T(8,128)(2,1)}) %reduce-scatter.5.cloned.1.call-update) | async-done | bytes 589840 | tf_op jit(solution)/shard_map/reduce_scatter | solution.py:134
  235.9 2.2 convert_element_type.489
  238.1 130.2 %all-reduce.5.cloned.1.call-done = f32[7,7,1536]{2,1,0:T(8,128)} async-done(((f32[7,7,1536]{2,1,0:T(8,128)}), f32[7,7,1536]{2,1,0:T(8,128)}) %all-reduce.5.cloned.1.call-update) | async-done | bytes 301072 | tf_op jit(solution)/shard_map/psum | solution.py:152
  368.3 1.7 copy.15
  (157 shorter events, 0.6 us)
Async XLA Ops:
  7.2 12.6 %copy-start = (bf16[1,3,16,1536]{3,2,1,0:T(8,128)(2,1)S(1)}, bf16[1,3,16,1536]{3,2,1,0:T(8,128)(2,1)}, u32[]{:S(2)}) copy-start(bf16[1,3,16,1536]{3,2,1,0:T(8,128)(2,1)} %param.10) | copy-start | bytes 442372
  7.2 12.8 %copy-start.52 = (f32[1536]{0:T(1024)S(1)}, f32[1536]{0:T(1024)}, u32[]{:S(2)}) copy-start(f32[1536]{0:T(1024)} %param.12) | copy-start | bytes 18436
  7.2 84.0 %all-gather.2.cloned.1.call-start = ((), (), s32[]{:S(2)}) async-start(), calls=%async_computation.2 | async-start | bytes 5308416 | tf_op jit(solution)/shard_map/all_gather | solution.py:108
  7.9 128.7 %reduce-scatter.3.cloned.1.call-start = ((), (), s32[]{:S(2)}) async-start(), calls=%async_computation.3 | async-start | bytes 737280 | tf_op jit(solution)/shard_map/reduce_scatter | solution.py:138
  8.0 11.7 %collective-permute-start.1 = (bf16[3,16,1536]{2,1,0:T(8,128)(2,1)}, bf16[3,16,1536]{2,1,0:T(8,128)(2,1)S(1)}, u32[]{:S(2)}, u32[]{:S(2)}) collective-permute-start(bf16[3,16,1536]{2,1,0:T(8,128)(2,1)} %bitcast.24), channel_id=1, source_target_pairs={{1,0},{2,1},{3,2},{5,4},{6,5},{7,6},{9,8},{10,9},{11,10},{13,12},{... | collective-permute-start | bytes 442376 | tf_op jit(solution)/shard_map/ppermute | solution.py:17
  9.9 9.8 %collective-permute-start = (bf16[3,16,1536]{2,1,0:T(8,128)(2,1)}, bf16[3,16,1536]{2,1,0:T(8,128)(2,1)S(1)}, u32[]{:S(2)}, u32[]{:S(2)}) collective-permute-start(bf16[3,16,1536]{2,1,0:T(8,128)(2,1)} %bitcast.25), channel_id=1, source_target_pairs={{0,1},{1,2},{2,3},{4,5},{5,6},{6,7},{8,9},{9,10},{10,11},{12,13},{... | collective-permute-start | bytes 442376 | tf_op jit(solution)/shard_map/ppermute | solution.py:14
  17.7 5.7 %copy-start.4 = (f32[1536]{0:T(1024)}, f32[1536]{0:T(1024)S(1)}, u32[]{:S(2)}) copy-start(f32[1536]{0:T(1024)S(1)} %get-tuple-element.99) | copy-start | bytes 18436
  17.7 5.7 %copy-start.6 = (f32[1536]{0:T(1024)}, f32[1536]{0:T(1024)S(1)}, u32[]{:S(2)}) copy-start(f32[1536]{0:T(1024)S(1)} %get-tuple-element.100) | copy-start | bytes 18436
  19.5 3.9 %copy-start.8 = (f32[1536]{0:T(1024)}, f32[1536]{0:T(1024)S(1)}, u32[]{:S(2)}) copy-start(f32[1536]{0:T(1024)S(1)} %get-tuple-element.71) | copy-start | bytes 18436
  19.5 3.9 %copy-start.10 = (f32[1536]{0:T(1024)}, f32[1536]{0:T(1024)S(1)}, u32[]{:S(2)}) copy-start(f32[1536]{0:T(1024)S(1)} %get-tuple-element.72) | copy-start | bytes 18436
  19.5 3.9 %copy-start.12 = (f32[1536]{0:T(1024)}, f32[1536]{0:T(1024)S(1)}, u32[]{:S(2)}) copy-start(f32[1536]{0:T(1024)S(1)} %get-tuple-element.73) | copy-start | bytes 18436
  19.5 3.9 %copy-start.14 = (f32[1536]{0:T(1024)}, f32[1536]{0:T(1024)S(1)}, u32[]{:S(2)}) copy-start(f32[1536]{0:T(1024)S(1)} %get-tuple-element.74) | copy-start | bytes 18436
  19.5 3.9 %copy-start.16 = (f32[1536]{0:T(1024)}, f32[1536]{0:T(1024)S(1)}, u32[]{:S(2)}) copy-start(f32[1536]{0:T(1024)S(1)} %get-tuple-element.75) | copy-start | bytes 18436
  19.6 3.9 %copy-start.18 = (f32[1536]{0:T(1024)}, f32[1536]{0:T(1024)S(1)}, u32[]{:S(2)}) copy-start(f32[1536]{0:T(1024)S(1)} %get-tuple-element.76) | copy-start | bytes 18436
  19.6 3.9 %copy-start.20 = (f32[1536]{0:T(1024)}, f32[1536]{0:T(1024)S(1)}, u32[]{:S(2)}) copy-start(f32[1536]{0:T(1024)S(1)} %get-tuple-element.77) | copy-start | bytes 18436
  19.6 3.9 %copy-start.22 = (f32[1536]{0:T(1024)}, f32[1536]{0:T(1024)S(1)}, u32[]{:S(2)}) copy-start(f32[1536]{0:T(1024)S(1)} %get-tuple-element.78) | copy-start | bytes 18436
  19.6 3.9 %copy-start.24 = (f32[1536]{0:T(1024)}, f32[1536]{0:T(1024)S(1)}, u32[]{:S(2)}) copy-start(f32[1536]{0:T(1024)S(1)} %get-tuple-element.79) | copy-start | bytes 18436
  19.6 3.9 %copy-start.26 = (f32[1536]{0:T(1024)}, f32[1536]{0:T(1024)S(1)}, u32[]{:S(2)}) copy-start(f32[1536]{0:T(1024)S(1)} %get-tuple-element.80) | copy-start | bytes 18436
  19.6 3.9 %copy-start.28 = (f32[1536]{0:T(1024)}, f32[1536]{0:T(1024)S(1)}, u32[]{:S(2)}) copy-start(f32[1536]{0:T(1024)S(1)} %get-tuple-element.81) | copy-start | bytes 18436
  19.6 3.9 %copy-start.30 = (f32[1536]{0:T(1024)}, f32[1536]{0:T(1024)S(1)}, u32[]{:S(2)}) copy-start(f32[1536]{0:T(1024)S(1)} %get-tuple-element.82) | copy-start | bytes 18436
  19.6 3.9 %copy-start.32 = (f32[1536]{0:T(1024)}, f32[1536]{0:T(1024)S(1)}, u32[]{:S(2)}) copy-start(f32[1536]{0:T(1024)S(1)} %get-tuple-element.83) | copy-start | bytes 18436
  19.6 3.9 %copy-start.34 = (f32[1536]{0:T(1024)}, f32[1536]{0:T(1024)S(1)}, u32[]{:S(2)}) copy-start(f32[1536]{0:T(1024)S(1)} %get-tuple-element.84) | copy-start | bytes 18436
  19.6 3.9 %copy-start.36 = (f32[1536]{0:T(1024)}, f32[1536]{0:T(1024)S(1)}, u32[]{:S(2)}) copy-start(f32[1536]{0:T(1024)S(1)} %get-tuple-element.85) | copy-start | bytes 18436
  19.7 3.9 %copy-start.38 = (f32[1536]{0:T(1024)}, f32[1536]{0:T(1024)S(1)}, u32[]{:S(2)}) copy-start(f32[1536]{0:T(1024)S(1)} %get-tuple-element.86) | copy-start | bytes 18436
  19.7 3.9 %copy-start.40 = (f32[1536]{0:T(1024)}, f32[1536]{0:T(1024)S(1)}, u32[]{:S(2)}) copy-start(f32[1536]{0:T(1024)S(1)} %get-tuple-element.87) | copy-start | bytes 18436
  19.7 3.9 %copy-start.42 = (f32[1536]{0:T(1024)}, f32[1536]{0:T(1024)S(1)}, u32[]{:S(2)}) copy-start(f32[1536]{0:T(1024)S(1)} %get-tuple-element.88) | copy-start | bytes 18436
  19.7 3.9 %copy-start.44 = (f32[1536]{0:T(1024)}, f32[1536]{0:T(1024)S(1)}, u32[]{:S(2)}) copy-start(f32[1536]{0:T(1024)S(1)} %get-tuple-element.89) | copy-start | bytes 18436
  20.0 4.8 %copy-start.3 = (f32[1536]{0:T(1024)S(1)}, f32[1536]{0:T(1024)}, u32[]{:S(2)}) copy-start(f32[1536]{0:T(1024)} %param.13) | copy-start | bytes 18436
  20.0 4.8 %copy-start.50 = (f32[1536]{0:T(1024)S(1)}, f32[1536]{0:T(1024)}, u32[]{:S(2)}) copy-start(f32[1536]{0:T(1024)} %param.14) | copy-start | bytes 18436
  23.6 67.6 %copy-start.1 = (bf16[1,12,16,1536]{3,2,1,0:T(8,128)(2,1)S(1)}, bf16[1,12,16,1536]{3,2,1,0:T(8,128)(2,1)}, u32[]{:S(2)}) copy-start(bf16[1,12,16,1536]{3,2,1,0:T(8,128)(2,1)} %param.19) | copy-start | bytes 1769476
  23.6 67.6 %copy-start.53 = (f32[1536]{0:T(1024)S(1)}, f32[1536]{0:T(1024)}, u32[]{:S(2)}) copy-start(f32[1536]{0:T(1024)} %param.16) | copy-start | bytes 18436
  91.2 7.4 %copy-start.2 = (f32[1536]{0:T(1024)S(1)}, f32[1536]{0:T(1024)}, u32[]{:S(2)}) copy-start(f32[1536]{0:T(1024)} %param.17) | copy-start | bytes 18436
  91.2 16.7 %copy-start.51 = (f32[1536]{0:T(1024)S(1)}, f32[1536]{0:T(1024)}, u32[]{:S(2)}) copy-start(f32[1536]{0:T(1024)} %param.18) | copy-start | bytes 18436
  116.0 119.9 %reduce-scatter.5.cloned.1.call-start = ((), (), s32[]{:S(2)}) async-start(), calls=%async_computation.4 | async-start | bytes 5308416 | tf_op jit(solution)/shard_map/reduce_scatter | solution.py:134
  119.6 17.0 %copy-start.47 = (f32[3,16]{1,0:T(4,128)S(1)}, f32[3,16]{1,0:T(4,128)}, u32[]{:S(2)}) copy-start(f32[3,16]{1,0:T(4,128)} %copy-done.46) | copy-start | bytes 580
  119.6 17.0 %copy-start.49 = (f32[3,16]{1,0:T(4,128)S(1)}, f32[3,16]{1,0:T(4,128)}, u32[]{:S(2)}) copy-start(f32[3,16]{1,0:T(4,128)} %copy-done.48) | copy-start | bytes 580
  119.6 248.7 %all-reduce.5.cloned.1.call-start = ((), (), s32[]{:S(2)}) async-start(), calls=%async_computation.5 | async-start | bytes 688128 | tf_op jit(solution)/shard_map/psum | solution.py:152
  139.6 9.3 %collective-permute-start.3 = (bf16[3,16,1536]{2,1,0:T(8,128)(2,1)S(1)}, bf16[3,16,1536]{2,1,0:T(8,128)(2,1)S(1)}, u32[]{:S(2)}, u32[]{:S(2)}) collective-permute-start(bf16[3,16,1536]{2,1,0:T(8,128)(2,1)S(1)} %get-tuple-element.118), channel_id=1, source_target_pairs={{1,0},{2,1},{3,2},{5,4},{6,5},{7,6},{9,8},{10,9},{11,10},{13,12},{... | collective-permute-start | bytes 442376 | tf_op jit(solution)/shard_map/ppermute | solution.py:17
  142.3 6.6 %collective-permute-start.2 = (bf16[3,16,1536]{2,1,0:T(8,128)(2,1)S(1)}, bf16[3,16,1536]{2,1,0:T(8,128)(2,1)S(1)}, u32[]{:S(2)}, u32[]{:S(2)}) collective-permute-start(bf16[3,16,1536]{2,1,0:T(8,128)(2,1)S(1)} %get-tuple-element.118), channel_id=1, source_target_pairs={{0,1},{1,2},{2,3},{4,5},{5,6},{6,7},{8,9},{9,10},{10,11},{12,13},{... | collective-permute-start | bytes 442376 | tf_op jit(solution)/shard_map/ppermute | solution.py:14
  147.9 1.3 copy-start.5
  147.9 1.3 copy-start.7
  147.9 1.3 copy-start.9
  147.9 1.3 copy-start.11
  147.9 1.3 copy-start.13
  147.9 1.3 copy-start.15
  147.9 1.3 copy-start.17
  147.9 1.3 copy-start.19
  148.0 1.3 copy-start.21
  (14 other events, 16.2 us)
Sparse Core Ops, SparseCore 0:
  10.2 80.9 all-gather.1
  116.1 20.4 reduce-scatter.2
  140.3 95.5 reduce-scatter.4
  241.7 126.5 all-reduce.4
where the time goes:
time: 377 us
  waiting for transfers between devices  291 us (77%)
  other arithmetic  17.4 us (5%)
  between operations  16.3 us (4%)
  matrix products  15.7 us (4%)
  blocking collectives  14.2 us (4%)
  starting transfers between devices  12.3 us (3%)
  local copies, waits for them, and re-layouts  9.57 us (3%)
    psum x1, waiting for transfers between devices, body(): kernel_total = lax.psum(kernel_local, ('fsdp', 'rows'))  130 us
    reduce_scatter x1, waiting for transfers between devices, body(): lax.psum_scatter(w_term.astype(jnp.bfloat16), 'fsdp', scatter_dimension=0...  83.8 us
    all_gather x1, waiting for transfers between devices, body(): columns = lax.all_gather(up_weight, 'fsdp', axis=0, tiled=True)  59.4 us
    reduce_scatter x1, waiting for transfers between devices, body(): lax.psum_scatter(jnp.einsum('hwf,cf->hwc', dpre_rows, columns, preferred_...  16.9 us
  transfers between devices with their start and end apart: 8, of which 4 were waited for; matrix products, arithmetic and copies ran while one was open for 6% of the time, Pallas kernels for 0%

commit v1 on v0

--- a/solution.py
+++ b/solution.py
@@ -4,6 +4,16 @@
 from jax.sharding import PartitionSpec as P
 
 FF = 6144
+
+
+def pass_along(x, name, dim):
+    size = lax.axis_size(name)
+    moving, pieces = (x, [x])
+    for _ in range(size - 1):
+        moving = lax.ppermute(moving, name, [(i, (i + 1) % size) for i in range(size)])
+        pieces.insert(0, moving)
+    flat = jnp.concatenate(pieces, axis=dim)
+    return jnp.roll(flat, (lax.axis_index(name) + 1) * x.shape[dim], axis=dim)
 
 
 def extended(block, sides, width):
@@ -105,7 +115,7 @@
 ):
     slab = frames[0]
     chans = slab.shape[2]
-    columns = lax.all_gather(up_weight, "fsdp", axis=0, tiled=True)
+    columns = pass_along(up_weight, "fsdp", 0)
     padded = extended(slab, (("rows", 0),), 3)
     activation_rows = conv_rows(padded, kernel, kernel_bias)
     normed_output, standardized_input, inverse_deviation = apply_layer_norm(

time: 377 us -> 404 us (1.072)
  blocking collectives: 14.2 us -> 24 us
  waiting for transfers between devices: 291 us -> 298 us
  local copies, waits for them, and re-layouts: 9.57 us -> 15.1 us
    ppermute x0 -> x7, waiting for transfers between devices: none -> 69.5 us  [pass_along(): lax.ppermute(moving, name, [(i, (i + 1) % size) for i in range(size)])]
    all_gather x1 -> x0, waiting for transfers between devices: 59.4 us -> none  [body(): columns = lax.all_gather(up_weight, 'fsdp', axis=0, tiled=True)]
    all_gather x1, blocking collectives: 6.86 us -> 12.4 us  [body(): whole = lax.all_gather(normed_output, 'rows', axis=0, tiled=True)]
    unnamed x109 -> x218, local copies, waits for them, and re-layouts: 2.91 us -> 7.55 us
    psum x1, blocking collectives: 7.32 us -> 11.6 us  [body(): norm_total = lax.psum(jnp.sum(norms), 'rows')]
  transfers between devices with their start and end apart: 8 -> 14, of which waited for: 4 -> 9; matrix products, arithmetic and copies ran while one was open for 6% -> 6% of each run, Pallas kernels for 0% -> 0%
where the time goes in v1:
time: 404 us; the launch traced here: 403 us
  waiting for transfers between devices  298 us (74%)
  blocking collectives  24 us (6%)
  other arithmetic  18.9 us (5%)
  between operations  17.1 us (4%)
  starting transfers between devices  15.8 us (4%)
  local copies, waits for them, and re-layouts  15.1 us (4%)
  matrix products  13.6 us (3%)
    psum x1, waiting for transfers between devices, body(): kernel_total = lax.psum(kernel_local, ('fsdp', 'rows'))  130 us
    reduce_scatter x1, waiting for transfers between devices, body(): lax.psum_scatter(w_term.astype(jnp.bfloat16), 'fsdp', scatter_dimension=0...  83.4 us
    ppermute x7, waiting for transfers between devices, pass_along(): lax.ppermute(moving, name, [(i, (i + 1) % size) for i in range(size)])  69.5 us
    reduce_scatter x1, waiting for transfers between devices, body(): lax.psum_scatter(jnp.einsum('hwf,cf->hwc', dpre_rows, columns, preferred_...  14.8 us
    all_gather x1, blocking collectives, body(): whole = lax.all_gather(normed_output, 'rows', axis=0, tiled=True)  12.4 us
    psum x1, blocking collectives, body(): norm_total = lax.psum(jnp.sum(norms), 'rows')  11.6 us
    ppermute x2, starting transfers between devices, extended(): lax.ppermute(lax.slice_in_dim(block, block.shape[dim] - width, None, axis...  8.68 us
  transfers between devices with their start and end apart: 14, of which 9 were waited for; matrix products, arithmetic and copies ran while one was open for 6% of the time, Pallas kernels for 0%

profile of v1, /device:TPU:1, one launch (start us, length us, event | category | flops | bytes accessed | tf_op | source)
XLA Modules:
  0.0 402.6 jit_solution(4147718608542229416)
XLA Ops:
  7.2 0.0 reduce-scatter.3.cloned.1.call-start
  7.2 2.1 collective-permute-start.2
  9.3 16.3 %collective-permute-done.2 = bf16[192,1536]{1,0:T(8,128)(2,1)S(1)} collective-permute-done((bf16[192,1536]{1,0:T(8,128)(2,1)}, bf16[192,1536]{1,0:T(8,128)(2,1)S(1)}, u32[]{:S(2)}, u32[]{:S(2)}) %collective-permute-start.2) | collective-permute-done | bytes 589856 | tf_op jit(solution)/shard_map/ppermute | solution.py:13
  25.7 16.3 %collective-permute-done.3 = bf16[192,1536]{1,0:T(8,128)(2,1)S(1)} collective-permute-done((bf16[192,1536]{1,0:T(8,128)(2,1)S(1)}, bf16[192,1536]{1,0:T(8,128)(2,1)S(1)}, u32[]{:S(2)}, u32[]{:S(2)}) %collective-permute-start.3) | collective-permute-done | bytes 589856 | tf_op jit(solution)/shard_map/ppermute | solution.py:13
  41.9 15.4 %collective-permute-done.4 = bf16[192,1536]{1,0:T(8,128)(2,1)S(1)} collective-permute-done((bf16[192,1536]{1,0:T(8,128)(2,1)S(1)}, bf16[192,1536]{1,0:T(8,128)(2,1)S(1)}, u32[]{:S(2)}, u32[]{:S(2)}) %collective-permute-start.4) | collective-permute-done | bytes 589856 | tf_op jit(solution)/shard_map/ppermute | solution.py:13
  57.3 5.7 %collective-permute-start = (bf16[3,16,1536]{2,1,0:T(8,128)(2,1)}, bf16[3,16,1536]{2,1,0:T(8,128)(2,1)S(1)}, u32[]{:S(2)}, u32[]{:S(2)}) collective-permute-start(bf16[3,16,1536]{2,1,0:T(8,128)(2,1)} %bitcast.23), channel_id=1, source_target_pairs={{0,1},{1,2},{2,3},{4,5},{5,6},{6,7},{8,9},{9,10},{10,11},{12,13},{... | collective-permute-start | bytes 442376 | tf_op jit(solution)/shard_map/ppermute | solution.py:24
  63.0 1.9 collective-permute-start.1
  65.0 6.8 %collective-permute-done.5 = bf16[192,1536]{1,0:T(8,128)(2,1)S(1)} collective-permute-done((bf16[192,1536]{1,0:T(8,128)(2,1)S(1)}, bf16[192,1536]{1,0:T(8,128)(2,1)S(1)}, u32[]{:S(2)}, u32[]{:S(2)}) %collective-permute-start.5) | collective-permute-done | bytes 589856 | tf_op jit(solution)/shard_map/ppermute | solution.py:13
  71.8 2.4 slice_reduce_fusion.48
  74.2 1.9 slice_reduce_fusion.46
  76.3 1.6 slice_reduce_fusion.47
  78.1 1.2 select_maximum_fusion.2
  79.4 6.0 %collective-permute-done.6 = bf16[192,1536]{1,0:T(8,128)(2,1)} collective-permute-done((bf16[192,1536]{1,0:T(8,128)(2,1)S(1)}, bf16[192,1536]{1,0:T(8,128)(2,1)}, u32[]{:S(2)}, u32[]{:S(2)}) %collective-permute-start.6) | collective-permute-done | bytes 589856 | tf_op jit(solution)/shard_map/ppermute | solution.py:13
  85.6 3.4 fusion.166
  89.3 0.2 multiply_reduce_fusion.2
  89.5 8.7 %collective-permute-done.7 = bf16[192,1536]{1,0:T(8,128)(2,1)S(1)} collective-permute-done((bf16[192,1536]{1,0:T(8,128)(2,1)}, bf16[192,1536]{1,0:T(8,128)(2,1)S(1)}, u32[]{:S(2)}, u32[]{:S(2)}) %collective-permute-start.7) | collective-permute-done | bytes 589856 | tf_op jit(solution)/shard_map/ppermute | solution.py:13
  98.2 0.1 add_convert_fusion.1
  98.4 12.4 %all_gather.3 = bf16[12,16,1536]{2,1,0:T(8,128)(2,1)S(1)} all-gather(bf16[3,16,1536]{2,1,0:T(8,128)(2,1)S(1)} %add_convert_fusion.1), channel_id=1, replica_groups=mesh['fsdp'=8,'rows'=4] {'rows'}, dimensions={0}, use_global_device_ids=true | all-gather | bytes 737280 | tf_op jit(solution)/shard_map/all_gather | solution.py:124
  110.9 1.2 constant_dynamic-update-slice_fusion.13
  112.1 0.0 copy-done.2
  112.3 1.0 copy-done
  113.4 1.1 constant_dynamic-update-slice_fusion.5
  114.8 1.0 copy-done.8
  115.8 5.2 %fusion.15 = (f32[1536]{0:T(1024)S(1)}, f32[1536]{0:T(1024)S(1)}, f32[192,1536]{1,0:T(8,128)S(1)}, f32[192,1536]{1,0:T(8,128)}) fusion(bf16[1,12,16,1536]{3,2,1,0:T(8,128)(2,1)S(1)} %copy-done.8, f32[1536]{0:T(1024)S(1)} %copy-done.100, bf16[192,1536]{1,0:T(8,128)(2,1)S(1)} %bitcast.20, bf16[3072,1536]{1,0:T(8,128)(2,1)S(1)} %constant_dynamic-update-slice_fusion, ...), kind=kOutput, calls=%fused_computation.68 | convolution fusion | flops 926610432 | bytes 8278020 | tf_op jit(solution)/shard_map/dot_general | solution.py:128
  121.0 0.6 copy-done.94
  121.6 0.6 multiply_reduce_fusion.3
  122.2 11.6 %all-reduce.2 = (f32[]{:T(128)}, f32[]{:T(128)}) all-reduce(f32[]{:T(128)} %get-tuple-element.115, f32[]{:T(128)} %get-tuple-element.114), channel_id=1, replica_groups=mesh['fsdp'=8,'rows'=4] {'rows'}, use_global_device_ids=true, to_apply=%region_4.5 | all-reduce | flops 2 | bytes 16 | tf_op jit(solution)/shard_map/psum | solution.py:133
  135.1 0.7 multiply_add_fusion
  135.8 3.1 fusion.14
  138.9 4.9 %fusion.8 = bf16[12,16,1536]{2,1,0:T(8,128)(2,1)} fusion(bf16[12,16,1536]{2,1,0:T(8,128)(2,1)S(1)} %bitcast.22, bf16[3072,1536]{1,0:T(8,128)(2,1)} %copy-done.93, s32[]{:T(128)S(6)} %select_n.14), kind=kOutput, calls=%fused_computation.57 | convolution fusion | flops 906264576 | bytes 5898244 | tf_op jit(solution)/shard_map/hwf,cf->hwc/dot_general | solution.py:149
  143.8 0.0 reduce-scatter.5.cloned.1.call-start
  143.9 3.6 convolution_convert_fusion
  147.5 0.2 all-reduce.5.cloned.1.call-start
  147.7 14.8 %reduce-scatter.3.cloned.1.call-done = bf16[3,16,1536]{2,1,0:T(8,128)(2,1)} async-done(((bf16[12,16,1536]{2,1,0:T(8,128)(2,1)}), bf16[3,16,1536]{2,1,0:T(8,128)(2,1)}) %reduce-scatter.3.cloned.1.call-update) | async-done | bytes 147472 | tf_op jit(solution)/shard_map/reduce_scatter | solution.py:148
  162.5 1.1 fusion.153
  163.6 1.9 fusion.151
  165.5 2.7 collective-permute-start.10
  168.2 3.0 collective-permute-start.9
  171.2 0.8 fusion.152
  172.0 0.6 fusion.142
  173.2 0.5 stack.199
  174.2 0.8 reshape.62
  175.0 0.2 select_maximum_fusion
  175.6 2.8 fusion.159
  178.4 83.4 %reduce-scatter.5.cloned.1.call-done = bf16[192,1536]{1,0:T(8,128)(2,1)} async-done(((bf16[1536,1536]{1,0:T(8,128)(2,1)}), bf16[192,1536]{1,0:T(8,128)(2,1)}) %reduce-scatter.5.cloned.1.call-update) | async-done | bytes 589840 | tf_op jit(solution)/shard_map/reduce_scatter | solution.py:144
  261.8 2.2 convert_element_type.489
  264.0 130.4 %all-reduce.5.cloned.1.call-done = f32[7,7,1536]{2,1,0:T(8,128)} async-done(((f32[7,7,1536]{2,1,0:T(8,128)}), f32[7,7,1536]{2,1,0:T(8,128)}) %all-reduce.5.cloned.1.call-update) | async-done | bytes 301072 | tf_op jit(solution)/shard_map/psum | solution.py:162
  394.3 1.7 copy.30
  (278 shorter events, 1.4 us)
Async XLA Ops:
  7.2 78.2 %copy-start.3 = (bf16[1,3,16,1536]{3,2,1,0:T(8,128)(2,1)S(1)}, bf16[1,3,16,1536]{3,2,1,0:T(8,128)(2,1)}, u32[]{:S(2)}) copy-start(bf16[1,3,16,1536]{3,2,1,0:T(8,128)(2,1)} %param.10) | copy-start | bytes 442372
  7.2 155.3 %reduce-scatter.3.cloned.1.call-start = ((), (), s32[]{:S(2)}) async-start(), calls=%async_computation.2 | async-start | bytes 737280 | tf_op jit(solution)/shard_map/reduce_scatter | solution.py:148
  7.2 18.4 %collective-permute-start.2 = (bf16[192,1536]{1,0:T(8,128)(2,1)}, bf16[192,1536]{1,0:T(8,128)(2,1)S(1)}, u32[]{:S(2)}, u32[]{:S(2)}) collective-permute-start(bf16[192,1536]{1,0:T(8,128)(2,1)} %param.15), channel_id=1, source_target_pairs={{0,4},{4,8},{8,12},{12,16},{16,20},{20,24},{24,28},{28,0},{1,5},{5... | collective-permute-start | bytes 1769480 | tf_op jit(solution)/shard_map/ppermute | solution.py:13
  25.6 16.3 %collective-permute-start.3 = (bf16[192,1536]{1,0:T(8,128)(2,1)S(1)}, bf16[192,1536]{1,0:T(8,128)(2,1)S(1)}, u32[]{:S(2)}, u32[]{:S(2)}) collective-permute-start(bf16[192,1536]{1,0:T(8,128)(2,1)S(1)} %collective-permute-done.2), channel_id=1, source_target_pairs={{0,4},{4,8},{8,12},{12,16},{16,20},{20,24},{24,28},{28,0},{1,5},{5... | collective-permute-start | bytes 1769480 | tf_op jit(solution)/shard_map/ppermute | solution.py:13
  41.9 15.4 %collective-permute-start.4 = (bf16[192,1536]{1,0:T(8,128)(2,1)S(1)}, bf16[192,1536]{1,0:T(8,128)(2,1)S(1)}, u32[]{:S(2)}, u32[]{:S(2)}) collective-permute-start(bf16[192,1536]{1,0:T(8,128)(2,1)S(1)} %collective-permute-done.3), channel_id=1, source_target_pairs={{0,4},{4,8},{8,12},{12,16},{16,20},{20,24},{24,28},{28,0},{1,5},{5... | collective-permute-start | bytes 1769480 | tf_op jit(solution)/shard_map/ppermute | solution.py:13
  57.3 14.4 %collective-permute-start.5 = (bf16[192,1536]{1,0:T(8,128)(2,1)S(1)}, bf16[192,1536]{1,0:T(8,128)(2,1)S(1)}, u32[]{:S(2)}, u32[]{:S(2)}) collective-permute-start(bf16[192,1536]{1,0:T(8,128)(2,1)S(1)} %collective-permute-done.4), channel_id=1, source_target_pairs={{0,4},{4,8},{8,12},{12,16},{16,20},{20,24},{24,28},{28,0},{1,5},{5... | collective-permute-start | bytes 1769480 | tf_op jit(solution)/shard_map/ppermute | solution.py:13
  57.3 20.8 %collective-permute-start = (bf16[3,16,1536]{2,1,0:T(8,128)(2,1)}, bf16[3,16,1536]{2,1,0:T(8,128)(2,1)S(1)}, u32[]{:S(2)}, u32[]{:S(2)}) collective-permute-start(bf16[3,16,1536]{2,1,0:T(8,128)(2,1)} %bitcast.23), channel_id=1, source_target_pairs={{0,1},{1,2},{2,3},{4,5},{5,6},{6,7},{8,9},{9,10},{10,11},{12,13},{... | collective-permute-start | bytes 442376 | tf_op jit(solution)/shard_map/ppermute | solution.py:24
  63.0 15.1 %collective-permute-start.1 = (bf16[3,16,1536]{2,1,0:T(8,128)(2,1)}, bf16[3,16,1536]{2,1,0:T(8,128)(2,1)S(1)}, u32[]{:S(2)}, u32[]{:S(2)}) collective-permute-start(bf16[3,16,1536]{2,1,0:T(8,128)(2,1)} %bitcast.24), channel_id=1, source_target_pairs={{1,0},{2,1},{3,2},{5,4},{6,5},{7,6},{9,8},{10,9},{11,10},{13,12},{... | collective-permute-start | bytes 442376 | tf_op jit(solution)/shard_map/ppermute | solution.py:27
  71.8 13.6 %copy-start.1 = (bf16[192,1536]{1,0:T(8,128)(2,1)}, bf16[192,1536]{1,0:T(8,128)(2,1)S(1)}, u32[]{:S(2)}) copy-start(bf16[192,1536]{1,0:T(8,128)(2,1)S(1)} %collective-permute-done.5) | copy-start | bytes 1769476
  71.8 13.6 %collective-permute-start.6 = (bf16[192,1536]{1,0:T(8,128)(2,1)S(1)}, bf16[192,1536]{1,0:T(8,128)(2,1)}, u32[]{:S(2)}, u32[]{:S(2)}) collective-permute-start(bf16[192,1536]{1,0:T(8,128)(2,1)S(1)} %collective-permute-done.5), channel_id=1, source_target_pairs={{0,4},{4,8},{8,12},{12,16},{16,20},{20,24},{24,28},{28,0},{1,5},{5... | collective-permute-start | bytes 1769480 | tf_op jit(solution)/shard_map/ppermute | solution.py:13
  74.2 14.9 %copy-start.11 = (f32[1536]{0:T(1024)}, f32[1536]{0:T(1024)S(1)}, u32[]{:S(2)}) copy-start(f32[1536]{0:T(1024)S(1)} %get-tuple-element.61) | copy-start | bytes 18436
  76.1 9.3 %copy-start.23 = (f32[1536]{0:T(1024)S(1)}, f32[1536]{0:T(1024)}, u32[]{:S(2)}) copy-start(f32[1536]{0:T(1024)} %get-tuple-element.67) | copy-start | bytes 18436
  76.1 9.3 %copy-start.25 = (f32[1536]{0:T(1024)S(1)}, f32[1536]{0:T(1024)}, u32[]{:S(2)}) copy-start(f32[1536]{0:T(1024)} %get-tuple-element.68) | copy-start | bytes 18436
  76.1 9.3 %copy-start.27 = (f32[1536]{0:T(1024)S(1)}, f32[1536]{0:T(1024)}, u32[]{:S(2)}) copy-start(f32[1536]{0:T(1024)} %get-tuple-element.69) | copy-start | bytes 18436
  76.1 9.3 %copy-start.29 = (f32[1536]{0:T(1024)S(1)}, f32[1536]{0:T(1024)}, u32[]{:S(2)}) copy-start(f32[1536]{0:T(1024)} %get-tuple-element.70) | copy-start | bytes 18436
  76.1 9.3 %copy-start.31 = (f32[1536]{0:T(1024)S(1)}, f32[1536]{0:T(1024)}, u32[]{:S(2)}) copy-start(f32[1536]{0:T(1024)} %get-tuple-element.90) | copy-start | bytes 18436
  76.2 9.3 %copy-start.33 = (f32[1536]{0:T(1024)S(1)}, f32[1536]{0:T(1024)}, u32[]{:S(2)}) copy-start(f32[1536]{0:T(1024)} %get-tuple-element.91) | copy-start | bytes 18436
  77.9 11.2 %copy-start.53 = (f32[1536]{0:T(1024)}, f32[1536]{0:T(1024)S(1)}, u32[]{:S(2)}) copy-start(f32[1536]{0:T(1024)S(1)} %get-tuple-element.71) | copy-start | bytes 18436
  77.9 11.2 %copy-start.55 = (f32[1536]{0:T(1024)}, f32[1536]{0:T(1024)S(1)}, u32[]{:S(2)}) copy-start(f32[1536]{0:T(1024)S(1)} %get-tuple-element.72) | copy-start | bytes 18436
  77.9 11.2 %copy-start.57 = (f32[1536]{0:T(1024)}, f32[1536]{0:T(1024)S(1)}, u32[]{:S(2)}) copy-start(f32[1536]{0:T(1024)S(1)} %get-tuple-element.73) | copy-start | bytes 18436
  77.9 11.1 %copy-start.59 = (f32[1536]{0:T(1024)}, f32[1536]{0:T(1024)S(1)}, u32[]{:S(2)}) copy-start(f32[1536]{0:T(1024)S(1)} %get-tuple-element.74) | copy-start | bytes 18436
  77.9 11.1 %copy-start.61 = (f32[1536]{0:T(1024)}, f32[1536]{0:T(1024)S(1)}, u32[]{:S(2)}) copy-start(f32[1536]{0:T(1024)S(1)} %get-tuple-element.75) | copy-start | bytes 18436
  77.9 11.1 %copy-start.63 = (f32[1536]{0:T(1024)}, f32[1536]{0:T(1024)S(1)}, u32[]{:S(2)}) copy-start(f32[1536]{0:T(1024)S(1)} %get-tuple-element.76) | copy-start | bytes 18436
  78.0 11.1 %copy-start.65 = (f32[1536]{0:T(1024)}, f32[1536]{0:T(1024)S(1)}, u32[]{:S(2)}) copy-start(f32[1536]{0:T(1024)S(1)} %get-tuple-element.77) | copy-start | bytes 18436
  78.0 11.1 %copy-start.67 = (f32[1536]{0:T(1024)}, f32[1536]{0:T(1024)S(1)}, u32[]{:S(2)}) copy-start(f32[1536]{0:T(1024)S(1)} %get-tuple-element.78) | copy-start | bytes 18436
  78.0 11.1 %copy-start.69 = (f32[1536]{0:T(1024)}, f32[1536]{0:T(1024)S(1)}, u32[]{:S(2)}) copy-start(f32[1536]{0:T(1024)S(1)} %get-tuple-element.79) | copy-start | bytes 18436
  78.0 11.1 %copy-start.71 = (f32[1536]{0:T(1024)}, f32[1536]{0:T(1024)S(1)}, u32[]{:S(2)}) copy-start(f32[1536]{0:T(1024)S(1)} %get-tuple-element.80) | copy-start | bytes 18436
  78.0 11.1 %copy-start.73 = (f32[1536]{0:T(1024)}, f32[1536]{0:T(1024)S(1)}, u32[]{:S(2)}) copy-start(f32[1536]{0:T(1024)S(1)} %get-tuple-element.81) | copy-start | bytes 18436
  78.0 11.1 %copy-start.75 = (f32[1536]{0:T(1024)}, f32[1536]{0:T(1024)S(1)}, u32[]{:S(2)}) copy-start(f32[1536]{0:T(1024)S(1)} %get-tuple-element.82) | copy-start | bytes 18436
  78.0 11.1 %copy-start.77 = (f32[1536]{0:T(1024)}, f32[1536]{0:T(1024)S(1)}, u32[]{:S(2)}) copy-start(f32[1536]{0:T(1024)S(1)} %get-tuple-element.83) | copy-start | bytes 18436
  78.0 11.1 %copy-start.79 = (f32[1536]{0:T(1024)}, f32[1536]{0:T(1024)S(1)}, u32[]{:S(2)}) copy-start(f32[1536]{0:T(1024)S(1)} %get-tuple-element.84) | copy-start | bytes 18436
  78.0 11.1 %copy-start.81 = (f32[1536]{0:T(1024)}, f32[1536]{0:T(1024)S(1)}, u32[]{:S(2)}) copy-start(f32[1536]{0:T(1024)S(1)} %get-tuple-element.85) | copy-start | bytes 18436
  78.0 11.1 %copy-start.83 = (f32[1536]{0:T(1024)}, f32[1536]{0:T(1024)S(1)}, u32[]{:S(2)}) copy-start(f32[1536]{0:T(1024)S(1)} %get-tuple-element.86) | copy-start | bytes 18436
  78.1 11.1 %copy-start.85 = (f32[1536]{0:T(1024)}, f32[1536]{0:T(1024)S(1)}, u32[]{:S(2)}) copy-start(f32[1536]{0:T(1024)S(1)} %get-tuple-element.87) | copy-start | bytes 18436
  78.1 11.1 %copy-start.87 = (f32[1536]{0:T(1024)}, f32[1536]{0:T(1024)S(1)}, u32[]{:S(2)}) copy-start(f32[1536]{0:T(1024)S(1)} %get-tuple-element.88) | copy-start | bytes 18436
  78.1 11.1 %copy-start.89 = (f32[1536]{0:T(1024)}, f32[1536]{0:T(1024)S(1)}, u32[]{:S(2)}) copy-start(f32[1536]{0:T(1024)S(1)} %get-tuple-element.89) | copy-start | bytes 18436
  78.1 11.1 %copy-start.4 = (bf16[3,16,1536]{2,1,0:T(8,128)(2,1)}, bf16[3,16,1536]{2,1,0:T(8,128)(2,1)S(1)}, u32[]{:S(2)}) copy-start(bf16[3,16,1536]{2,1,0:T(8,128)(2,1)S(1)} %collective-permute-done) | copy-start | bytes 442372
  78.1 11.1 %copy-start.6 = (bf16[3,16,1536]{2,1,0:T(8,128)(2,1)}, bf16[3,16,1536]{2,1,0:T(8,128)(2,1)S(1)}, u32[]{:S(2)}) copy-start(bf16[3,16,1536]{2,1,0:T(8,128)(2,1)S(1)} %collective-permute-done.1) | copy-start | bytes 442372
  85.4 12.8 %collective-permute-start.7 = (bf16[192,1536]{1,0:T(8,128)(2,1)}, bf16[192,1536]{1,0:T(8,128)(2,1)S(1)}, u32[]{:S(2)}, u32[]{:S(2)}) collective-permute-start(bf16[192,1536]{1,0:T(8,128)(2,1)} %collective-permute-done.6), channel_id=1, source_target_pairs={{0,4},{4,8},{8,12},{12,16},{16,20},{20,24},{24,28},{28,0},{1,5},{5... | collective-permute-start | bytes 1769480 | tf_op jit(solution)/shard_map/ppermute | solution.py:13
  85.6 12.6 %copy-start.10 = (f32[1536]{0:T(1024)S(1)}, f32[1536]{0:T(1024)}, u32[]{:S(2)}) copy-start(f32[1536]{0:T(1024)} %param.13) | copy-start | bytes 18436
  85.6 12.6 %copy-start.98 = (f32[1536]{0:T(1024)S(1)}, f32[1536]{0:T(1024)}, u32[]{:S(2)}) copy-start(f32[1536]{0:T(1024)} %param.14) | copy-start | bytes 18436
  98.2 12.6 %collective-permute-start.8 = (bf16[192,1536]{1,0:T(8,128)(2,1)S(1)}, bf16[192,1536]{1,0:T(8,128)(2,1)S(1)}, u32[]{:S(2)}, u32[]{:S(2)}) collective-permute-start(bf16[192,1536]{1,0:T(8,128)(2,1)S(1)} %collective-permute-done.7), channel_id=1, source_target_pairs={{0,4},{4,8},{8,12},{12,16},{16,20},{20,24},{24,28},{28,0},{1,5},{5... | collective-permute-start | bytes 1769480 | tf_op jit(solution)/shard_map/ppermute | solution.py:13
  143.8 118.0 %reduce-scatter.5.cloned.1.call-start = ((), (), s32[]{:S(2)}) async-start(), calls=%async_computation.3 | async-start | bytes 5308416 | tf_op jit(solution)/shard_map/reduce_scatter | solution.py:144
  147.4 15.1 %copy-start.92 = (f32[3,16]{1,0:T(4,128)S(1)}, f32[3,16]{1,0:T(4,128)}, u32[]{:S(2)}) copy-start(f32[3,16]{1,0:T(4,128)} %copy-done.91) | copy-start | bytes 580
  147.4 15.1 %copy-start.97 = (f32[3,16]{1,0:T(4,128)S(1)}, f32[3,16]{1,0:T(4,128)}, u32[]{:S(2)}) copy-start(f32[3,16]{1,0:T(4,128)} %copy-done.96) | copy-start | bytes 580
  147.5 246.9 %all-reduce.5.cloned.1.call-start = ((), (), s32[]{:S(2)}) async-start(), calls=%async_computation.4 | async-start | bytes 688128 | tf_op jit(solution)/shard_map/psum | solution.py:162
  165.5 9.5 %collective-permute-start.10 = (bf16[3,16,1536]{2,1,0:T(8,128)(2,1)S(1)}, bf16[3,16,1536]{2,1,0:T(8,128)(2,1)S(1)}, u32[]{:S(2)}, u32[]{:S(2)}) collective-permute-start(bf16[3,16,1536]{2,1,0:T(8,128)(2,1)S(1)} %get-tuple-element.118), channel_id=1, source_target_pairs={{1,0},{2,1},{3,2},{5,4},{6,5},{7,6},{9,8},{10,9},{11,10},{13,12},{... | collective-permute-start | bytes 442376 | tf_op jit(solution)/shard_map/ppermute | solution.py:27
  168.2 6.8 %collective-permute-start.9 = (bf16[3,16,1536]{2,1,0:T(8,128)(2,1)S(1)}, bf16[3,16,1536]{2,1,0:T(8,128)(2,1)S(1)}, u32[]{:S(2)}, u32[]{:S(2)}) collective-permute-start(bf16[3,16,1536]{2,1,0:T(8,128)(2,1)S(1)} %get-tuple-element.118), channel_id=1, source_target_pairs={{0,1},{1,2},{2,3},{4,5},{5,6},{6,7},{8,9},{9,10},{10,11},{12,13},{... | collective-permute-start | bytes 442376 | tf_op jit(solution)/shard_map/ppermute | solution.py:24
  (67 other events, 247.1 us)
Sparse Core Ops, SparseCore 0:
  143.9 18.5 reduce-scatter.2
  166.1 95.5 reduce-scatter.4
  267.7 126.6 all-reduce.4
